TPU v7x, 128 devices: a whole 4x4x4 slice. The times are simulated.
128 devices in a mesh: dp: 8 (over z, core), ts: 16 (over y, x).
Axes of the slice: x: 4, y: 4, z: 4, core: 2. Of those that a mesh axis runs over, the one named last changes fastest.
Arguments:
- text_embed: bfloat16 [8, 1024, 4096], P('dp', None, 'ts'), may hold values from -6 to 6
- bridge: bfloat16 [128, 32, 4096], P('dp', None, 'ts'), may hold values from -6 to 6
- crystal_slot: int32 [128], P('dp'), may hold values from 0 to 8159, as said below
- segments: int32 [8, 1024], P('dp'), may hold values from 0 to 15, as said below
- attn_gain: float32 [4096], replicated, may hold values from 0.1 to 1.9
- w_query: bfloat16 [4096, 4096], P(None, 'ts'), as said below
- w_key: bfloat16 [4096, 1024], P(None, 'ts'), may hold values from -0.09375 to 0.09375
- w_value: bfloat16 [4096, 1024], P(None, 'ts'), may hold values from -0.09375 to 0.09375
- w_out: bfloat16 [4096, 4096], P('ts'), may hold values from -0.09375 to 0.09375
- mlp_gain: float32 [4096], replicated, may hold values from 0.1 to 1.9
- w_gate: bfloat16 [4096, 12288], P(None, 'ts'), may hold values from -0.09375 to 0.09375
- w_up: bfloat16 [4096, 12288], P(None, 'ts'), may hold values from -0.09375 to 0.09375
- w_down: bfloat16 [12288, 4096], P('ts'), may hold values from -0.0546875 to 0.0546875
Outputs:
- layer_out: bfloat16 [8, 1024, 4096], P('dp', 'ts')
Inputs may be any that keep to these rules, and one draw needn't show every extreme that they name: `segments`: each row starts at 0, never falls and names every document number of 0 to 15; every document holds at least 33 positions. `crystal_slot`: each crystal's 32 rows take the first 32 positions of one document, given as sequence * 1024 + that document's first position; every document takes exactly one crystal, and each sequence takes exactly 2 of the 16 crystals held by each index of dp. `w_query`: entries lie within plus or minus 104 / sqrt(4096).
All inputs are finite; a program needn't handle non-finite values.
Results may differ from a plain program's by a relative error of at most 0.025.
The roundings to bfloat16 on the way count: a program that leaves them out, or rounds other values in their place, can miss the bound.
Values may be sent and summed in bfloat16 or wider, within the bound.
No kernel may reach another device: no remote copies, remote signals or barrier semaphores. Data moves between devices by JAX's collectives and lax.ppermute only.
A program may use at most 128 MiB of HBM per device.

v0:
```python
import jax
import jax.numpy as jnp
from jax import lax
from jax.sharding import PartitionSpec as P

HD = 128
DOC_LEN = 64
norm_epsilon = 1e-05
rope_base = 500000.0
masked_score = -1e30


def partner_2(block, axis, apart):
    count = lax.axis_size(axis)
    route = []
    for low in range(count):
        high = low | 1 << apart
        if high != low and high < count:
            route += [(low, high), (high, low)]
    return lax.ppermute(block, axis, route)


def norm_rows(rows, gain):
    widened = rows.astype(jnp.float32)
    inverse_rms = lax.rsqrt(jnp.mean(widened * widened, axis=-1, keepdims=True) + norm_epsilon)
    return (widened * inverse_rms * gain).astype(jnp.bfloat16)


def rotate_pairs(values, positions, first_pair):
    pair_count = values.shape[-1] // 2
    exponent = 2.0 * (first_pair + jnp.arange(pair_count, dtype=jnp.int32)).astype(jnp.float32) / HD
    frequency = rope_base ** (-exponent)
    angles = positions.astype(jnp.float32)[:, None] * frequency[None, :]
    cosine = jnp.cos(angles)[:, None, :]
    sine_part = jnp.sin(angles)[:, None, :]
    paired = values.reshape(values.shape[0], values.shape[1], pair_count, 2)
    even_part = paired[..., 0]
    odd_part = paired[..., 1]
    new_even = even_part * cosine - odd_part * sine_part
    new_odd = even_part * sine_part + odd_part * cosine
    return jnp.stack([new_even, new_odd], axis=-1).reshape(values.shape)


def attend_block(query_block, query_segments, query_index, keys_full, values_full, segment_ids):
    scores = jnp.einsum(
        "qhd,kd->hqk", query_block, keys_full, preferred_element_type=jnp.float32
    ) * HD ** (-0.5)
    key_index = jnp.arange(keys_full.shape[0], dtype=jnp.int32)
    allowed = (query_segments[:, None] == segment_ids[None, :]) & (
        key_index[None, :] <= query_index[:, None]
    )
    scores = jnp.where(allowed[None], scores, masked_score)
    row_top = jnp.max(scores, axis=-1, keepdims=True)
    weights = jnp.exp(scores - row_top)
    probabilities = (weights / jnp.sum(weights, axis=-1, keepdims=True)).astype(jnp.bfloat16)
    mixed_rows = jnp.einsum(
        "hqk,kd->qhd", probabilities, values_full, preferred_element_type=jnp.float32
    )
    return mixed_rows.astype(jnp.bfloat16).reshape(query_block.shape[0], -1)


def shards(
    text_embed,
    bridge,
    crystal_slot,
    segments,
    attn_gain,
    w_query,
    w_key,
    w_value,
    w_out,
    mlp_gain,
    w_gate,
    w_up,
    w_down,
):
    seq_len = text_embed.shape[1]
    part_width = text_embed.shape[2]
    doc_count = seq_len // DOC_LEN
    bridge_len = bridge.shape[1]
    tok_rows = seq_len // lax.axis_size("ts")
    group_index = lax.axis_index("dp")
    ts_index = lax.axis_index("ts")
    segment_ids = segments[0]
    doc_numbers = jnp.arange(doc_count, dtype=jnp.int32)
    starts = jnp.sum((segment_ids[None, :] < doc_numbers[:, None]).astype(jnp.int32), axis=1)
    doc_match = segment_ids[:, None] == doc_numbers[None, :]
    positions = jnp.arange(seq_len, dtype=jnp.int32) - jnp.sum(
        jnp.where(doc_match, starts[None, :], 0), axis=1
    )
    flat_bridge = bridge.reshape(bridge.shape[0], bridge_len * part_width)
    arrived, arrived_slots = (
        lax.all_gather(flat_bridge, "dp", axis=0, tiled=True),
        lax.all_gather(crystal_slot, "dp", axis=0, tiled=True),
    )
    wanted = group_index * seq_len + starts
    picking = wanted[:, None] == arrived_slots[None, :]
    by_doc = jnp.dot(
        picking.astype(jnp.bfloat16), arrived, preferred_element_type=jnp.float32
    ).astype(jnp.bfloat16)
    by_doc = by_doc.reshape(doc_count * bridge_len, part_width)
    in_bridge = positions < bridge_len
    row_pick = (segment_ids * bridge_len + positions)[:, None] == jnp.arange(
        doc_count * bridge_len, dtype=jnp.int32
    )[None, :]
    row_pick = row_pick & in_bridge[:, None]
    filled = jnp.dot(
        row_pick.astype(jnp.bfloat16), by_doc, preferred_element_type=jnp.float32
    ).astype(jnp.bfloat16)
    own_part = jnp.where(in_bridge[:, None], filled, text_embed[0])
    packed = lax.all_gather(own_part, "ts", axis=1, tiled=True)
    normed = norm_rows(packed, attn_gain)
    heads_here = w_query.shape[1] // HD
    queries = jnp.dot(normed, w_query, preferred_element_type=jnp.float32).reshape(
        seq_len, heads_here, HD
    )
    queries = rotate_pairs(queries, positions, 0).astype(jnp.bfloat16)
    kv_cols = w_key.shape[1]
    upper_half = ts_index % 2 == 1
    key_half = jnp.dot(normed, w_key, preferred_element_type=jnp.float32).reshape(
        seq_len, 1, kv_cols
    )
    key_half = rotate_pairs(key_half, positions, ts_index % 2 * (kv_cols // 2))
    key_half = key_half.astype(jnp.bfloat16).reshape(seq_len, kv_cols)
    value_half = jnp.dot(normed, w_value, preferred_element_type=jnp.float32).astype(jnp.bfloat16)
    own_pair = jnp.concatenate([key_half, value_half], axis=1)
    partner = partner_2(own_pair, "ts", 0)
    lower_half = jnp.where(upper_half, partner, own_pair)
    higher = jnp.where(upper_half, own_pair, partner)
    keys_full = jnp.concatenate([lower_half[:, :kv_cols], higher[:, :kv_cols]], axis=1)
    values_full = jnp.concatenate([lower_half[:, kv_cols:], higher[:, kv_cols:]], axis=1)
    block_rows = min(512, seq_len)
    outputs = []
    for block_index in range(seq_len // block_rows):
        first_row = block_index * block_rows
        query_index = jnp.arange(first_row, first_row + block_rows, dtype=jnp.int32)
        outputs.append(
            attend_block(
                queries[first_row : first_row + block_rows],
                segment_ids[first_row : first_row + block_rows],
                query_index,
                keys_full,
                values_full,
                segment_ids,
            )
        )
    attended = jnp.concatenate(outputs, axis=0)
    mine_offset = ts_index * tok_rows
    partial_rows = jnp.dot(attended, w_out, preferred_element_type=jnp.float32)
    attn_sum = lax.psum(partial_rows.astype(jnp.bfloat16), "ts").astype(jnp.float32)
    after_all = (packed.astype(jnp.float32) + attn_sum).astype(jnp.bfloat16)
    after_mine = lax.dynamic_slice_in_dim(after_all, mine_offset, tok_rows, 0)
    normed_mlp = norm_rows(after_all, mlp_gain)
    gate_proj = jnp.dot(normed_mlp, w_gate, preferred_element_type=jnp.float32)
    up_proj = jnp.dot(normed_mlp, w_up, preferred_element_type=jnp.float32)
    hidden = (jax.nn.silu(gate_proj) * up_proj).astype(jnp.bfloat16)
    mlp_mine = lax.psum_scatter(
        jnp.dot(hidden, w_down, preferred_element_type=jnp.float32).astype(jnp.bfloat16),
        "ts",
        scatter_dimension=0,
        tiled=True,
    ).astype(jnp.float32)
    layer_rows = (after_mine.astype(jnp.float32) + mlp_mine).astype(jnp.bfloat16)
    return layer_rows.reshape(1, tok_rows, layer_rows.shape[1])


def solution(mesh):
    return jax.shard_map(
        shards,
        mesh=mesh,
        in_specs=(
            P("dp", None, "ts"),
            P("dp", None, "ts"),
            P("dp"),
            P("dp", None),
            P(),
            P(None, "ts"),
            P(None, "ts"),
            P(None, "ts"),
            P("ts", None),
            P(),
            P(None, "ts"),
            P(None, "ts"),
            P("ts", None),
        ),
        out_specs=P("dp", "ts", None),
        check_vma=False,
    )
```

profile of v0, /device:TPU:0, one launch (start us, length us, event | category | flops | bytes accessed | tf_op | source)
XLA Modules:
  0.0 462.7 jit_solution(8637387790045024165)
XLA Ops:
  11.4 10.6 %all-reduce = s32[128]{0:T(128)S(1)} all-reduce(s32[128]{0:T(128)S(1)} %dynamic-update-slice), channel_id=1, replica_groups=mesh['dp'=8,'ts'=16] {'dp'}, use_global_device_ids=true, to_apply=%add | all-reduce | flops 128 | bytes 1024
  24.3 12.6 %all-gather.3.cloned.1.call-done = bf16[128,8192]{1,0:T(8,128)(2,1)} async-done(((bf16[16,8192]{1,0:T(8,128)(2,1)}), bf16[128,8192]{1,0:T(8,128)(2,1)}) %all-gather.3.cloned.1.call-update) | async-done | bytes 2097168 | tf_op jit(solution)/shard_map/all_gather | solution.py:93
  37.0 2.0 convolution_convert_fusion
  39.1 2.7 fusion.36
  42.0 2.3 multiply_cosine_fusion
  45.9 74.7 %all-gather.5.cloned.1.call-done = bf16[1024,4096]{1,0:T(8,128)(2,1)} async-done(((bf16[1024,256]{1,0:T(8,128)(2,1)}), bf16[1024,4096]{1,0:T(8,128)(2,1)}) %all-gather.5.cloned.1.call-update) | async-done | bytes 8388624 | tf_op jit(solution)/shard_map/all_gather | solution.py:111
  120.6 5.1 %fusion.5 = f32[1024]{0:T(1024)S(1)} fusion(bf16[1024,4096]{1,0:T(8,128)(2,1)} %all-gather.5.cloned.1.call-done), kind=kLoop, calls=%fused_computation.10 | loop fusion | flops 12581888 | bytes 8392704 | tf_op jit(solution)/shard_map/reduce_sum | solution.py:25
  125.7 10.4 %fusion.7 = bf16[1024,4096]{1,0:T(8,128)(2,1)} fusion(bf16[1024,4096]{1,0:T(8,128)(2,1)} %all-gather.5.cloned.1.call-done, f32[4096]{0:T(1024)S(1)} %copy-done.8, f32[1024]{0:T(1024)S(1)} %add_rsqrt_fusion.1), kind=kLoop, calls=%fused_computation.12 | loop fusion | flops 16777216 | bytes 16797696 | tf_op jit(solution)/shard_map/convert_element_type | solution.py:26
  136.1 6.2 %convolution_convert_fusion.3 = bf16[1024,64]{0,1:T(8,128)(2,1)S(1)} fusion(bf16[1024,4096]{1,0:T(8,128)(2,1)} %fusion.7, bf16[4096,64]{0,1:T(8,128)(2,1)S(1)} %copy-done.4), kind=kOutput, calls=%fused_computation.48 | convolution fusion | flops 536936448 | bytes 9043968 | tf_op jit(solution)/shard_map/dot_general | solution.py:125
  142.4 2.7 fusion.103
  145.0 3.6 fusion.104
  155.5 2.1 subtract_convert_fusion
  158.9 2.7 collective-permute-done
  161.7 4.8 %fusion.98 = (f32[2,512]{1,0:T(2,128)S(1)}, f32[2,512,1024]{1,2,0:T(8,128)}) fusion(pred[512,1024]{0,1:T(8,128)(4,1)} %get-tuple-element.25, bf16[512,2,128]{0,1,2:T(2,128)(2,1)} %bitcast.86, bf16[1024,64]{0,1:T(8,128)(2,1)S(1)} %get-tuple-element.35, bf16[1024,64]{0,1:T(8,128)(2,1)S(1)} %get-tuple-element.18), kind=kOutput, calls=%fused_computation.119 | convolution fusion | flops 273155072 | bytes 5246976 | tf_op jit(solution)/shard_map/sub | solution.py:54
  166.5 3.7 fusion.93
  170.2 2.8 fusion.40
  174.2 5.6 %convolution_convert_fusion.2 = bf16[1024,4096]{1,0:T(8,128)(2,1)} fusion(bf16[256,4096]{1,0:T(8,128)(2,1)S(1)} %copy-done, bf16[512,256]{0,1:T(8,128)(2,1)S(1)} %bitcast.83, bf16[512,256]{0,1:T(8,128)(2,1)S(1)} %bitcast.82), kind=kOutput, calls=%fused_computation.16 | convolution fusion | flops 2152726528 | bytes 11010048 | tf_op jit(solution)/shard_map/dot_general | solution.py:149
  179.8 140.8 %all-reduce.3.cloned.1.call-done = bf16[1024,4096]{1,0:T(8,128)(2,1)} async-done(((bf16[1024,4096]{1,0:T(8,128)(2,1)}), bf16[1024,4096]{1,0:T(8,128)(2,1)}) %all-reduce.3.cloned.1.call-update) | async-done | bytes 8388624 | tf_op jit(solution)/shard_map/psum | solution.py:150
  320.6 8.0 %fusion.2 = (f32[1024]{0:T(1024)S(1)}, bf16[1024,4096]{1,0:T(8,128)(2,1)S(1)}) fusion(bf16[1024,4096]{1,0:T(8,128)(2,1)} %all-reduce.3.cloned.1.call-done, bf16[1024,4096]{1,0:T(8,128)(2,1)} %all-gather.5.cloned.1.call-done), kind=kLoop, calls=%fused_computation.7 | loop fusion | flops 29359104 | bytes 25169920 | tf_op jit(solution)/shard_map/reduce_sum | solution.py:25
  328.7 3.2 copy-done.3
  331.9 11.3 %fusion.11 = f32[1024,768]{1,0:T(8,128)} fusion(bf16[4096,768]{1,0:T(8,128)(2,1)} %param.24, bf16[1024,4096]{1,0:T(8,128)(2,1)S(1)} %get-tuple-element.6, f32[4096]{0:T(1024)S(1)} %copy-done.10, f32[1024]{0:T(1024)S(1)} %add_rsqrt_fusion), kind=kOutput, calls=%fused_computation.26 | convolution fusion | flops 6459228160 | bytes 17846272 | tf_op jit(solution)/shard_map/dot_general | solution.py:155
  343.2 26.4 %convolution_convert_fusion.1 = bf16[1024,4096]{1,0:T(8,128)(2,1)} fusion(bf16[768,4096]{1,0:T(8,128)(2,1)} %param.25, f32[1024,768]{1,0:T(8,128)} %fusion.11, bf16[4096,768]{1,0:T(8,128)(2,1)} %param.23, bf16[1024,4096]{1,0:T(8,128)(2,1)} %copy-done.3, f32[4096]{0:T(1024)S(1)} %copy-done.10, f32[1024]{0:T(1024)S(1)} %add_rsqrt_fusion), kind=kOutput, calls=%fused_computation.15 | convolution fusion | flops 12910592000 | bytes 32526336 | tf_op jit(solution)/shard_map/dot_general | solution.py:158
  369.6 84.2 %reduce-scatter.2.cloned.1.call-done = bf16[64,4096]{1,0:T(8,128)(2,1)} async-done(((bf16[1024,4096]{1,0:T(8,128)(2,1)}), bf16[64,4096]{1,0:T(8,128)(2,1)}) %reduce-scatter.2.cloned.1.call-update) | async-done | bytes 524304 | tf_op jit(solution)/shard_map/reduce_scatter | solution.py:157
  453.8 2.1 fusion.43
  (62 shorter events, 17.8 us)
Async XLA Ops:
  6.5 167.6 %copy-start = (bf16[256,4096]{1,0:T(8,128)(2,1)S(1)}, bf16[256,4096]{1,0:T(8,128)(2,1)}, u32[]{:S(2)}) copy-start(bf16[256,4096]{1,0:T(8,128)(2,1)} %param.21) | copy-start | bytes 6291460
  6.5 35.4 %copy-start.7 = (s32[1,1024]{1,0:T(1,128)S(1)}, s32[1,1024]{1,0:T(1,128)}, u32[]{:S(2)}) copy-start(s32[1,1024]{1,0:T(1,128)} %param.16) | copy-start | bytes 12292
  6.5 30.4 %all-gather.3.cloned.1.call-start = ((), (), s32[]{:S(2)}) async-start(), calls=%async_computation.1 | async-start | bytes 2359296 | tf_op jit(solution)/shard_map/all_gather | solution.py:93
  8.5 112.1 %all-gather.5.cloned.1.call-start = ((), (), s32[]{:S(2)}) async-start(), calls=%async_computation.2 | async-start | bytes 8912896 | tf_op jit(solution)/shard_map/all_gather | solution.py:111
  39.1 86.6 %copy-start.8 = (f32[4096]{0:T(1024)S(1)}, f32[4096]{0:T(1024)}, u32[]{:S(2)}) copy-start(f32[4096]{0:T(1024)} %param.17) | copy-start | bytes 49156
  41.9 278.8 %all-reduce.3.cloned.1.call-start = ((), (), s32[]{:S(2)}) async-start(), calls=%async_computation.3 | async-start | bytes 16777216 | tf_op jit(solution)/shard_map/psum | solution.py:150
  125.7 10.4 %copy-start.4 = (bf16[4096,64]{0,1:T(8,128)(2,1)S(1)}, bf16[4096,64]{0,1:T(8,128)(2,1)}, u32[]{:S(2)}) copy-start(bf16[4096,64]{0,1:T(8,128)(2,1)} %param.20) | copy-start | bytes 1572868
  136.1 6.2 %copy-start.2 = (bf16[1024,4096]{1,0:T(8,128)(2,1)S(1)}, bf16[1024,4096]{1,0:T(8,128)(2,1)}, u32[]{:S(2)}) copy-start(bf16[1024,4096]{1,0:T(8,128)(2,1)} %fusion.7) | copy-start | bytes 25165828
  136.1 6.2 %copy-start.5 = (bf16[4096,64]{0,1:T(8,128)(2,1)S(1)}, bf16[4096,64]{0,1:T(8,128)(2,1)}, u32[]{:S(2)}) copy-start(bf16[4096,64]{0,1:T(8,128)(2,1)} %param.19) | copy-start | bytes 1572868
  142.3 2.7 copy-start.9
  154.3 7.3 %collective-permute-start = (bf16[1024,128]{0,1:T(8,128)(2,1)S(1)}, bf16[1024,128]{0,1:T(8,128)(2,1)S(1)}, u32[]{:S(2)}, u32[]{:S(2)}) collective-permute-start(bf16[1024,128]{0,1:T(8,128)(2,1)S(1)} %pad_maximum_fusion.1), channel_id=1, source_target_pairs={{0,1},{1,0},{2,3},{3,2},{4,5},{5,4},{6,7},{7,6},{8,9},{9,8},{10,11... | collective-permute-start | bytes 786440 | tf_op jit(solution)/shard_map/ppermute | solution.py:20
  157.6 8.9 %copy-start.6 = (pred[512,1024]{0,1:T(8,128)(4,1)S(1)}, pred[512,1024]{0,1:T(8,128)(4,1)}, u32[]{:S(2)}) copy-start(pred[512,1024]{0,1:T(8,128)(4,1)} %get-tuple-element.26) | copy-start | bytes 1572868
  170.2 3.4 copy-start.11
  179.8 152.1 %copy-start.10 = (f32[4096]{0:T(1024)S(1)}, f32[4096]{0:T(1024)}, u32[]{:S(2)}) copy-start(f32[4096]{0:T(1024)} %param.22) | copy-start | bytes 49156
  179.8 274.0 %reduce-scatter.2.cloned.1.call-start = ((), (), s32[]{:S(2)}) async-start(), calls=%async_computation.4 | async-start | bytes 8912896 | tf_op jit(solution)/shard_map/reduce_scatter | solution.py:157
  328.7 3.2 copy-start.3
  343.2 112.7 %copy-start.1 = (bf16[256,4096]{1,0:T(8,128)(2,1)S(1)}, bf16[256,4096]{1,0:T(8,128)(2,1)}, u32[]{:S(2)}) copy-start(bf16[256,4096]{1,0:T(8,128)(2,1)} %param.21) | copy-start | bytes 6291460
Sparse Core Ops, SparseCore 0:
  9.1 27.8 all-gather.2
  42.0 78.5 all-gather.4
  179.9 140.6 all-reduce.2
  369.7 84.0 reduce-scatter.1
where the time goes:
time: 466 us; the launch traced here: 463 us
  waiting for transfers between devices  315 us (68%)
  matrix products  72.3 us (16%)
  other arithmetic  35.9 us (8%)
  between operations  14.3 us (3%)
  local copies, waits for them, and re-layouts  13.2 us (3%)
  blocking collectives  10.6 us (2%)
    psum x1, waiting for transfers between devices, shards(): lax.psum(partial_rows.astype(jnp.bfloat16), 'ts').astype(jnp.float32)  141 us
    reduce_scatter x1, waiting for transfers between devices, shards(): lax.psum_scatter(jnp.dot(hidden, w_down, preferred_element_type=jnp.float...  84.2 us
    all_gather x1, waiting for transfers between devices, shards(): packed = lax.all_gather(own_part, 'ts', axis=1, tiled=True)  74.7 us
    dot_general x1, matrix products, shards(): jnp.dot(hidden, w_down, preferred_element_type=jnp.float32)  26.4 us
    reduce_sum x2, other arithmetic, norm_rows(): jnp.mean(widened * widened, axis=-1, keepdims=True) + norm_epsilon  13.1 us
    all_gather x1, waiting for transfers between devices, shards(): lax.all_gather(flat_bridge, 'dp', axis=0, tiled=True)  12.6 us
    dot_general x1, matrix products, shards(): up_proj = jnp.dot(normed_mlp, w_up, preferred_element_type=jnp.float32)  11.3 us
    unnamed x1, blocking collectives  10.6 us
  transfers between devices with their start and end apart: 5, of which 5 were waited for; matrix products, arithmetic and copies ran while one was open for 3% of the time, Pallas kernels for 0%

commit v1 on v0

--- a/solution.py
+++ b/solution.py
@@ -8,6 +8,28 @@
 norm_epsilon = 1e-05
 rope_base = 500000.0
 masked_score = -1e30
+
+
+def laid_out(pieces, dim):
+    pieces = jnp.moveaxis(pieces, 0, dim)
+    dims = pieces.shape
+    return pieces.reshape(*dims[:dim], dims[dim] * dims[dim + 1], *dims[dim + 2 :])
+
+
+def gather_around(x, axis, dim):
+    peers = lax.axis_size(axis)
+    pairs = [(i, (i + 1) % peers) for i in range(peers)]
+    back = [(b, a) for a, b in pairs]
+    lower, upper = ([], [])
+    for step in range(peers - 1):
+        if step % 2 == 0:
+            lower.append(lax.ppermute(lower[-1] if lower else x, axis, pairs))
+        else:
+            upper.append(lax.ppermute(upper[-1] if upper else x, axis, back))
+    blocks = jnp.stack([*lower[::-1], x, *upper])
+    shift = lax.axis_index(axis) - len(lower)
+    blocks = blocks[(jnp.arange(peers) - shift) % peers]
+    return laid_out(blocks, dim)
 
 
 def partner_2(block, axis, apart):
@@ -90,7 +112,7 @@
     )
     flat_bridge = bridge.reshape(bridge.shape[0], bridge_len * part_width)
     arrived, arrived_slots = (
-        lax.all_gather(flat_bridge, "dp", axis=0, tiled=True),
+        gather_around(flat_bridge, "dp", 0),
         lax.all_gather(crystal_slot, "dp", axis=0, tiled=True),
     )
     wanted = group_index * seq_len + starts

time: 466 us -> 484 us (1.039)
  local copies, waits for them, and re-layouts: 13.2 us -> 25.5 us
  starting transfers between devices: 1.38 us -> 7.91 us
    ppermute x0 -> x7, waiting for transfers between devices: none -> 13.6 us  [the longest x4 13.5 us: gather_around(): lower.append(lax.ppermute(lower[-1] if lower else x, axis, pairs))]
    all_gather x1 -> x0, waiting for transfers between devices: 12.6 us -> none  [shards(): lax.all_gather(flat_bridge, 'dp', axis=0, tiled=True)]
    ppermute x0 -> x7, starting transfers between devices: none -> 6.57 us  [the longest x3 6.54 us: gather_around(): upper.append(lax.ppermute(upper[-1] if upper else x, axis, back))]
    unnamed x28 -> x41, local copies, waits for them, and re-layouts: 8.03 us -> 14.2 us
  transfers between devices with their start and end apart: 5 -> 11, of which waited for: 5 -> 7; matrix products, arithmetic and copies ran while one was open for 3% -> 4% of each run, Pallas kernels for 0% -> 0%
where the time goes in v1:
time: 484 us; the launch traced here: 481 us
  waiting for transfers between devices  314 us (65%)
  matrix products  73.2 us (15%)
  other arithmetic  36 us (7%)
  local copies, waits for them, and re-layouts  25.5 us (5%)
  between operations  14.3 us (3%)
  blocking collectives  9.31 us (2%)
  starting transfers between devices  7.91 us (2%)
    psum x1, waiting for transfers between devices, shards(): lax.psum(partial_rows.astype(jnp.bfloat16), 'ts').astype(jnp.float32)  141 us
    reduce_scatter x1, waiting for transfers between devices, shards(): lax.psum_scatter(jnp.dot(hidden, w_down, preferred_element_type=jnp.float...  84 us
    all_gather x1, waiting for transfers between devices, shards(): packed = lax.all_gather(own_part, 'ts', axis=1, tiled=True)  73.4 us
    dot_general x1, matrix products, shards(): jnp.dot(hidden, w_down, preferred_element_type=jnp.float32)  26.3 us
    unnamed x41, local copies, waits for them, and re-layouts  14.2 us
    ppermute x4, waiting for transfers between devices, gather_around(): lower.append(lax.ppermute(lower[-1] if lower else x, axis, pairs))  13.5 us
    reduce_sum x2, other arithmetic, norm_rows(): jnp.mean(widened * widened, axis=-1, keepdims=True) + norm_epsilon  13.1 us
    dot_general x1, matrix products, shards(): up_proj = jnp.dot(normed_mlp, w_up, preferred_element_type=jnp.float32)  11.3 us
  transfers between devices with their start and end apart: 11, of which 7 were waited for; matrix products, arithmetic and copies ran while one was open for 4% of the time, Pallas kernels for 0%

profile of v1, /device:TPU:0, one launch (start us, length us, event | category | flops | bytes accessed | tf_op | source)
XLA Modules:
  0.0 480.6 jit_solution(363233375653968150)
XLA Ops:
  7.8 3.6 collective-permute-start.4
  12.2 3.2 collective-permute-done
  16.2 6.2 %collective-permute-done.1 = bf16[16,8192]{1,0:T(8,128)(2,1)S(1)} collective-permute-done((bf16[16,8192]{1,0:T(8,128)(2,1)S(1)}, bf16[16,8192]{1,0:T(8,128)(2,1)S(1)}, u32[]{:S(2)}, u32[]{:S(2)}) %collective-permute-start.1) | collective-permute-done | bytes 262176 | tf_op jit(solution)/shard_map/ppermute | solution.py:26
  22.5 3.0 collective-permute-start.5
  25.4 4.1 collective-permute-done.2
  33.4 9.3 %all-reduce = s32[128]{0:T(128)S(1)} all-reduce(s32[128]{0:T(128)S(1)} %dynamic-update-slice), channel_id=1, replica_groups=mesh['dp'=8,'ts'=16] {'dp'}, use_global_device_ids=true, to_apply=%add | all-reduce | flops 128 | bytes 1024
  51.1 3.6 gather_fusion
  56.9 2.7 fusion.36
  63.7 73.4 %all-gather.2.cloned.1.call-done = bf16[1024,4096]{1,0:T(8,128)(2,1)} async-done(((bf16[1024,256]{1,0:T(8,128)(2,1)}), bf16[1024,4096]{1,0:T(8,128)(2,1)}) %all-gather.2.cloned.1.call-update) | async-done | bytes 8388624 | tf_op jit(solution)/shard_map/all_gather | solution.py:133
  137.1 5.1 %fusion.5 = f32[1024]{0:T(1024)S(1)} fusion(bf16[1024,4096]{1,0:T(8,128)(2,1)} %all-gather.2.cloned.1.call-done), kind=kLoop, calls=%fused_computation.11 | loop fusion | flops 12581888 | bytes 8392704 | tf_op jit(solution)/shard_map/reduce_sum | solution.py:47
  142.2 10.4 %fusion.7 = bf16[1024,4096]{1,0:T(8,128)(2,1)} fusion(bf16[1024,4096]{1,0:T(8,128)(2,1)} %all-gather.2.cloned.1.call-done, f32[4096]{0:T(1024)S(1)} %copy-done.11, f32[1024]{0:T(1024)S(1)} %add_rsqrt_fusion.1), kind=kLoop, calls=%fused_computation.13 | loop fusion | flops 16777216 | bytes 16797696 | tf_op jit(solution)/shard_map/convert_element_type | solution.py:48
  152.6 6.2 %convolution_convert_fusion.3 = bf16[1024,64]{0,1:T(8,128)(2,1)S(1)} fusion(bf16[1024,4096]{1,0:T(8,128)(2,1)} %fusion.7, bf16[4096,64]{0,1:T(8,128)(2,1)S(1)} %copy-done.4), kind=kOutput, calls=%fused_computation.49 | convolution fusion | flops 536936448 | bytes 9043968 | tf_op jit(solution)/shard_map/dot_general | solution.py:147
  158.8 2.7 fusion.105
  161.5 3.6 fusion.106
  178.9 4.9 %fusion.100 = (f32[2,512]{1,0:T(2,128)S(1)}, f32[2,512,1024]{1,2,0:T(8,128)}) fusion(pred[512,1024]{0,1:T(8,128)(4,1)S(1)} %copy-done.7, bf16[512,2,128]{0,1,2:T(2,128)(2,1)} %bitcast.105, bf16[1024,64]{0,1:T(8,128)(2,1)} %get-tuple-element.35, bf16[1024,64]{0,1:T(8,128)(2,1)} %get-tuple-element.18), kind=kOutput, calls=%fused_computation.135 | convolution fusion | flops 273155072 | bytes 5246976 | tf_op jit(solution)/shard_map/sub | solution.py:76
  183.8 4.7 fusion.95
  188.4 2.8 fusion.40
  192.4 5.6 %convolution_convert_fusion.2 = bf16[1024,4096]{1,0:T(8,128)(2,1)} fusion(bf16[256,4096]{1,0:T(8,128)(2,1)S(1)} %copy-done, bf16[512,256]{0,1:T(8,128)(2,1)S(1)} %bitcast.101, bf16[512,256]{0,1:T(8,128)(2,1)S(1)} %bitcast.100), kind=kOutput, calls=%fused_computation.17 | convolution fusion | flops 2152726528 | bytes 11010048 | tf_op jit(solution)/shard_map/dot_general | solution.py:171
  198.1 140.8 %all-reduce.3.cloned.1.call-done = bf16[1024,4096]{1,0:T(8,128)(2,1)} async-done(((bf16[1024,4096]{1,0:T(8,128)(2,1)}), bf16[1024,4096]{1,0:T(8,128)(2,1)}) %all-reduce.3.cloned.1.call-update) | async-done | bytes 8388624 | tf_op jit(solution)/shard_map/psum | solution.py:172
  338.9 8.0 %fusion.2 = (f32[1024]{0:T(1024)S(1)}, bf16[1024,4096]{1,0:T(8,128)(2,1)S(1)}) fusion(bf16[1024,4096]{1,0:T(8,128)(2,1)} %all-reduce.3.cloned.1.call-done, bf16[1024,4096]{1,0:T(8,128)(2,1)} %all-gather.2.cloned.1.call-done), kind=kLoop, calls=%fused_computation.8 | loop fusion | flops 29359104 | bytes 25169920 | tf_op jit(solution)/shard_map/reduce_sum | solution.py:47
  346.9 3.2 copy-done.3
  350.1 11.3 %fusion.11 = f32[1024,768]{1,0:T(8,128)} fusion(bf16[4096,768]{1,0:T(8,128)(2,1)} %param.24, bf16[1024,4096]{1,0:T(8,128)(2,1)S(1)} %get-tuple-element.6, f32[4096]{0:T(1024)S(1)} %copy-done.13, f32[1024]{0:T(1024)S(1)} %add_rsqrt_fusion), kind=kOutput, calls=%fused_computation.27 | convolution fusion | flops 6459228160 | bytes 17846272 | tf_op jit(solution)/shard_map/dot_general | solution.py:177
  361.4 26.3 %convolution_convert_fusion.1 = bf16[1024,4096]{1,0:T(8,128)(2,1)} fusion(bf16[768,4096]{1,0:T(8,128)(2,1)} %param.25, f32[1024,768]{1,0:T(8,128)} %fusion.11, bf16[4096,768]{1,0:T(8,128)(2,1)} %param.23, bf16[1024,4096]{1,0:T(8,128)(2,1)} %copy-done.3, f32[4096]{0:T(1024)S(1)} %copy-done.13, f32[1024]{0:T(1024)S(1)} %add_rsqrt_fusion), kind=kOutput, calls=%fused_computation.16 | convolution fusion | flops 12910592000 | bytes 32526336 | tf_op jit(solution)/shard_map/dot_general | solution.py:180
  387.7 84.0 %reduce-scatter.2.cloned.1.call-done = bf16[64,4096]{1,0:T(8,128)(2,1)} async-done(((bf16[1024,4096]{1,0:T(8,128)(2,1)}), bf16[64,4096]{1,0:T(8,128)(2,1)}) %reduce-scatter.2.cloned.1.call-update) | async-done | bytes 524304 | tf_op jit(solution)/shard_map/reduce_scatter | solution.py:179
  (91 shorter events, 37.7 us)
Async XLA Ops:
  6.5 185.8 %copy-start = (bf16[256,4096]{1,0:T(8,128)(2,1)S(1)}, bf16[256,4096]{1,0:T(8,128)(2,1)}, u32[]{:S(2)}) copy-start(bf16[256,4096]{1,0:T(8,128)(2,1)} %param.21) | copy-start | bytes 6291460
  6.5 130.5 %all-gather.2.cloned.1.call-start = ((), (), s32[]{:S(2)}) async-start(), calls=%async_computation.1 | async-start | bytes 8912896 | tf_op jit(solution)/shard_map/all_gather | solution.py:133
  7.8 7.6 %collective-permute-start = (bf16[16,8192]{1,0:T(8,128)(2,1)S(1)}, bf16[16,8192]{1,0:T(8,128)(2,1)S(1)}, u32[]{:S(2)}, u32[]{:S(2)}) collective-permute-start(bf16[16,8192]{1,0:T(8,128)(2,1)S(1)} %bitcast.102), channel_id=1, source_target_pairs={{0,16},{16,32},{32,48},{48,64},{64,80},{80,96},{96,112},{112,0},{1... | collective-permute-start | bytes 786440 | tf_op jit(solution)/shard_map/ppermute | solution.py:26
  7.8 14.6 %collective-permute-start.4 = (bf16[16,8192]{1,0:T(8,128)(2,1)S(1)}, bf16[16,8192]{1,0:T(8,128)(2,1)S(1)}, u32[]{:S(2)}, u32[]{:S(2)}) collective-permute-start(bf16[16,8192]{1,0:T(8,128)(2,1)S(1)} %bitcast.103), channel_id=1, source_target_pairs={{16,0},{32,16},{48,32},{64,48},{80,64},{96,80},{112,96},{0,112},{1... | collective-permute-start | bytes 786440 | tf_op jit(solution)/shard_map/ppermute | solution.py:28
  15.4 7.0 %collective-permute-start.1 = (bf16[16,8192]{1,0:T(8,128)(2,1)S(1)}, bf16[16,8192]{1,0:T(8,128)(2,1)S(1)}, u32[]{:S(2)}, u32[]{:S(2)}) collective-permute-start(bf16[16,8192]{1,0:T(8,128)(2,1)S(1)} %collective-permute-done), channel_id=1, source_target_pairs={{0,16},{16,32},{32,48},{48,64},{64,80},{80,96},{96,112},{112,0},{1... | collective-permute-start | bytes 786440 | tf_op jit(solution)/shard_map/ppermute | solution.py:26
  22.4 7.1 %collective-permute-start.2 = (bf16[16,8192]{1,0:T(8,128)(2,1)S(1)}, bf16[16,8192]{1,0:T(8,128)(2,1)}, u32[]{:S(2)}, u32[]{:S(2)}) collective-permute-start(bf16[16,8192]{1,0:T(8,128)(2,1)S(1)} %collective-permute-done.1), channel_id=1, source_target_pairs={{0,16},{16,32},{32,48},{48,64},{64,80},{80,96},{96,112},{112,0},{1... | collective-permute-start | bytes 786440 | tf_op jit(solution)/shard_map/ppermute | solution.py:26
  22.5 20.9 %collective-permute-start.5 = (bf16[16,8192]{1,0:T(8,128)(2,1)S(1)}, bf16[16,8192]{1,0:T(8,128)(2,1)S(1)}, u32[]{:S(2)}, u32[]{:S(2)}) collective-permute-start(bf16[16,8192]{1,0:T(8,128)(2,1)S(1)} %collective-permute-done.4), channel_id=1, source_target_pairs={{16,0},{32,16},{48,32},{64,48},{80,64},{96,80},{112,96},{0,112},{1... | collective-permute-start | bytes 786440 | tf_op jit(solution)/shard_map/ppermute | solution.py:28
  29.5 13.9 %collective-permute-start.3 = (bf16[16,8192]{1,0:T(8,128)(2,1)}, bf16[16,8192]{1,0:T(8,128)(2,1)}, u32[]{:S(2)}, u32[]{:S(2)}) collective-permute-start(bf16[16,8192]{1,0:T(8,128)(2,1)} %collective-permute-done.2), channel_id=1, source_target_pairs={{0,16},{16,32},{32,48},{48,64},{64,80},{80,96},{96,112},{112,0},{1... | collective-permute-start | bytes 786440 | tf_op jit(solution)/shard_map/ppermute | solution.py:26
  43.4 7.0 %collective-permute-start.6 = (bf16[16,8192]{1,0:T(8,128)(2,1)S(1)}, bf16[16,8192]{1,0:T(8,128)(2,1)S(1)}, u32[]{:S(2)}, u32[]{:S(2)}) collective-permute-start(bf16[16,8192]{1,0:T(8,128)(2,1)S(1)} %collective-permute-done.5), channel_id=1, source_target_pairs={{16,0},{32,16},{48,32},{64,48},{80,64},{96,80},{112,96},{0,112},{1... | collective-permute-start | bytes 786440 | tf_op jit(solution)/shard_map/ppermute | solution.py:28
  51.1 8.6 %copy-start.10 = (s32[1,1024]{1,0:T(1,128)S(1)}, s32[1,1024]{1,0:T(1,128)}, u32[]{:S(2)}) copy-start(s32[1,1024]{1,0:T(1,128)} %param.16) | copy-start | bytes 12292
  59.6 279.2 %all-reduce.3.cloned.1.call-start = ((), (), s32[]{:S(2)}) async-start(), calls=%async_computation.2 | async-start | bytes 16777216 | tf_op jit(solution)/shard_map/psum | solution.py:172
  63.7 78.5 %copy-start.11 = (f32[4096]{0:T(1024)S(1)}, f32[4096]{0:T(1024)}, u32[]{:S(2)}) copy-start(f32[4096]{0:T(1024)} %param.17) | copy-start | bytes 49156
  142.2 10.4 %copy-start.4 = (bf16[4096,64]{0,1:T(8,128)(2,1)S(1)}, bf16[4096,64]{0,1:T(8,128)(2,1)}, u32[]{:S(2)}) copy-start(bf16[4096,64]{0,1:T(8,128)(2,1)} %param.20) | copy-start | bytes 1572868
  152.6 6.2 %copy-start.2 = (bf16[1024,4096]{1,0:T(8,128)(2,1)S(1)}, bf16[1024,4096]{1,0:T(8,128)(2,1)}, u32[]{:S(2)}) copy-start(bf16[1024,4096]{1,0:T(8,128)(2,1)} %fusion.7) | copy-start | bytes 25165828
  152.6 6.2 %copy-start.5 = (bf16[4096,64]{0,1:T(8,128)(2,1)S(1)}, bf16[4096,64]{0,1:T(8,128)(2,1)}, u32[]{:S(2)}) copy-start(bf16[4096,64]{0,1:T(8,128)(2,1)} %param.19) | copy-start | bytes 1572868
  170.7 8.2 %copy-start.7 = (pred[512,1024]{0,1:T(8,128)(4,1)S(1)}, pred[512,1024]{0,1:T(8,128)(4,1)}, u32[]{:S(2)}) copy-start(pred[512,1024]{0,1:T(8,128)(4,1)} %get-tuple-element.25) | copy-start | bytes 1572868
  170.8 7.3 %collective-permute-start.7 = (bf16[1024,128]{0,1:T(8,128)(2,1)S(1)}, bf16[1024,128]{0,1:T(8,128)(2,1)S(1)}, u32[]{:S(2)}, u32[]{:S(2)}) collective-permute-start(bf16[1024,128]{0,1:T(8,128)(2,1)S(1)} %pad_maximum_fusion.1), channel_id=1, source_target_pairs={{0,1},{1,0},{2,3},{3,2},{4,5},{5,4},{6,7},{7,6},{8,9},{9,8},{10,11... | collective-permute-start | bytes 786440 | tf_op jit(solution)/shard_map/ppermute | solution.py:42
  178.9 4.9 %copy-start.6 = (pred[512,1024]{0,1:T(8,128)(4,1)S(1)}, pred[512,1024]{0,1:T(8,128)(4,1)}, u32[]{:S(2)}) copy-start(pred[512,1024]{0,1:T(8,128)(4,1)} %get-tuple-element.26) | copy-start | bytes 1572868
  178.9 4.9 %copy-start.8 = (bf16[512,2,64,2]{0,1,3,2:T(2,128)(2,1)S(1)}, bf16[512,2,64,2]{0,1,3,2:T(2,128)(2,1)}, u32[]{:S(2)}) copy-start(bf16[512,2,64,2]{0,1,3,2:T(2,128)(2,1)} %get-tuple-element.12) | copy-start | bytes 786436
  183.8 4.7 copy-start.9
  188.4 3.4 copy-start.14
  198.0 152.1 %copy-start.13 = (f32[4096]{0:T(1024)S(1)}, f32[4096]{0:T(1024)}, u32[]{:S(2)}) copy-start(f32[4096]{0:T(1024)} %param.22) | copy-start | bytes 49156
  198.0 273.7 %reduce-scatter.2.cloned.1.call-start = ((), (), s32[]{:S(2)}) async-start(), calls=%async_computation.3 | async-start | bytes 8912896 | tf_op jit(solution)/shard_map/reduce_scatter | solution.py:179
  387.6 86.2 %copy-start.1 = (bf16[256,4096]{1,0:T(8,128)(2,1)S(1)}, bf16[256,4096]{1,0:T(8,128)(2,1)}, u32[]{:S(2)}) copy-start(bf16[256,4096]{1,0:T(8,128)(2,1)} %param.21) | copy-start | bytes 6291460
  (2 other events, 5.9 us)
Sparse Core Ops, SparseCore 0:
  59.8 77.2 all-gather.1
  198.1 140.6 all-reduce.2
  387.8 83.8 reduce-scatter.1
